TPU v7x, 32 devices: a whole 2x2x4 slice. The times are simulated.
32 devices in a mesh: section: 4 (over z), dp: 2 (over core), seq: 4 (over y, x).
Axes of the slice: x: 2, y: 2, z: 4, core: 2. Of those that a mesh axis runs over, the one named last changes fastest.
Arguments:
- qkv: bfloat16 [4, 4, 256, 6144], P('section', 'dp', 'seq'), may hold values from -5 to 5
- stream_lengths: int32 [4, 4], P('section'), may hold values from 1 to 192, 256 in all within a row
- doc_lengths: int32 [4, 4, 8], P('section'), may hold values from 1 to 128, 256 in all within a row
- hand_over: int32 [4, 2], P('section'), may hold values from 0 to 1
Outputs:
- handoff: bfloat16 [4, 4, 256, 4096], P('section', 'dp', 'seq')
Inputs may be any that keep to these rules, and one draw needn't show every extreme that they name: `stream_lengths`: each entry is the length of one row; the 4 entries of one section, taken together, sum to 256, and in each section one entry is exactly the most.
All inputs are finite; a program needn't handle non-finite values.
Results may differ from a plain program's by a relative error of at most 0.0013.
Values may be sent and summed in bfloat16 or wider, within the bound.
No kernel may reach another device: no remote copies, remote signals or barrier semaphores. Data moves between devices by JAX's collectives and lax.ppermute only.
A program may use at most 64 MiB of HBM per device.

v0:
```python
import jax
import jax.numpy as jnp
from jax import lax
from jax.sharding import PartitionSpec as P

H = 32
HD = 128
KV_HEADS = 8
D = 4096
RPR = 2


def swapped(block, axis, distance):
    count = lax.axis_size(axis)
    route = []
    for low in range(count):
        high = low | 1 << distance
        if high != low and high < count:
            route += [(low, high), (high, low)]
    return lax.ppermute(block, axis, route)


def passed_along(value, axis, steps):
    count = lax.axis_size(axis)
    pairs = [(source, (source + steps) % count) for source in range(count)]
    return lax.ppermute(value, axis, pairs)


def attend(row_data, row_ids, stream_lengths, doc_ends, seq_count):
    seg_len = row_data.shape[1]
    length = seg_len * seq_count
    heads_dev = H // seq_count
    group_size = H // KV_HEADS
    kv_dev = max(1, heads_dev // group_size)
    copies = max(1, group_size // heads_dev)
    group_local = heads_dev // kv_dev
    q_width = H * HD
    key_value_width = KV_HEADS * HD
    query_send = row_data[..., :q_width].reshape(RPR, seg_len, seq_count, heads_dev * HD)
    key_portion = row_data[..., q_width : q_width + key_value_width]
    value_part = row_data[..., q_width + key_value_width :]
    key_send = jnp.repeat(key_portion.reshape(RPR, seg_len, KV_HEADS, HD), copies, axis=2).reshape(
        RPR, seg_len, seq_count, kv_dev * HD
    )
    value_send = jnp.repeat(value_part.reshape(RPR, seg_len, KV_HEADS, HD), copies, axis=2).reshape(
        RPR, seg_len, seq_count, kv_dev * HD
    )
    query_heads, kv_heads = (
        lax.all_to_all(query_send, "seq", split_axis=2, concat_axis=1, tiled=True),
        lax.all_to_all(
            jnp.concatenate([key_send, value_send], axis=3),
            "seq",
            split_axis=2,
            concat_axis=1,
            tiled=True,
        ),
    )
    key_block = kv_heads[:, :, 0, : kv_dev * HD]
    value_block = kv_heads[:, :, 0, kv_dev * HD :]
    query_tile_rows = query_heads[:, :, 0, :]
    positions = jnp.arange(length, dtype=jnp.int32)
    row_match = (
        jnp.arange(doc_ends.shape[0], dtype=jnp.int32)[None, :] == row_ids[:, None]
    ).astype(jnp.int32)
    ends_rows = jnp.sum(row_match[:, :, None] * doc_ends[None, :, :], axis=1)
    lengths_rows = jnp.sum(row_match * stream_lengths[None, :], axis=1)
    doc_index = jnp.sum(
        (positions[None, :, None] >= ends_rows[:, None, :]).astype(jnp.int32), axis=2
    )
    causal = positions[:, None] >= positions[None, :]
    score_scale = HD ** (-0.5)
    results = []
    for slot_index in range(RPR):
        allowed = causal & (doc_index[slot_index][:, None] == doc_index[slot_index][None, :])
        query_row = query_tile_rows[slot_index].reshape(length, kv_dev, group_local, HD)
        key_row = key_block[slot_index].reshape(length, kv_dev, HD)
        value_row = value_block[slot_index].reshape(length, kv_dev, HD)
        scores = (
            jnp.einsum("qkgd,skd->kgqs", query_row, key_row, preferred_element_type=jnp.float32)
            * score_scale
        )
        row_top = jnp.max(jnp.where(allowed, scores, -jnp.inf), axis=-1, keepdims=True)
        weights = jnp.where(allowed, jnp.exp(scores - row_top), 0.0)
        row_total = jnp.sum(weights, axis=-1)
        rounded = weights.astype(jnp.bfloat16)
        summed = jnp.einsum(
            "kgqs,skd->qkgd", rounded, value_row, preferred_element_type=jnp.float32
        )
        result = summed / jnp.transpose(row_total, (2, 0, 1))[..., None]
        valid = (positions < lengths_rows[slot_index]).astype(jnp.float32)
        result = result * valid[:, None, None, None]
        results.append(result.reshape(length, heads_dev * HD).astype(jnp.bfloat16))
    return jnp.stack(results, axis=0)


def shards(qkv, stream_lengths, doc_lengths, hand_over):
    seq_count = lax.axis_size("seq")
    replica = lax.axis_index("dp")
    partner = jnp.bitwise_xor(replica, 1)
    handed = lax.dynamic_index_in_dim(hand_over[0], replica, 0, keepdims=False)
    partner_handed = lax.dynamic_index_in_dim(hand_over[0], partner, 0, keepdims=False)
    own_rows = qkv[0]
    seg_len = own_rows.shape[1]
    doc_ends = jnp.cumsum(doc_lengths[0], axis=1)
    lengths_all = stream_lengths[0]
    given = lax.dynamic_index_in_dim(own_rows, handed, 0, keepdims=True)
    kept = lax.dynamic_index_in_dim(own_rows, 1 - handed, 0, keepdims=True)
    received = swapped(given, "dp", 0)
    row_ids = jnp.stack([2 * replica + 1 - handed, 2 * partner + partner_handed])
    attention_output = attend(
        jnp.concatenate([kept, received], axis=0), row_ids, lengths_all, doc_ends, seq_count
    )
    grouped = attention_output.reshape(RPR, seq_count, seg_len, attention_output.shape[2])
    tokens = lax.all_to_all(grouped, "seq", split_axis=1, concat_axis=3, tiled=True)
    tokens = passed_along(tokens, "section", 1)
    return tokens.reshape(1, RPR, seg_len, D)


def solution(mesh):
    return jax.shard_map(
        shards,
        mesh=mesh,
        in_specs=(
            P("section", "dp", "seq", None),
            P("section", None),
            P("section", None, None),
            P("section", None),
        ),
        out_specs=P("section", "dp", "seq", None),
        check_vma=False,
    )
```

profile of v0, /device:TPU:0, one launch (start us, length us, event | category | flops | bytes accessed | tf_op | source)
XLA Modules:
  0.0 89.6 jit_solution(12574448168181887721)
XLA Ops:
  0.0 0.0 copy-start
  0.0 0.0 copy-start.1
  0.0 1.4 %constant_dynamic-slice_fusion = (s32[1,1]{1,0:T(1,128)}, s32[1,1]{1,0:T(1,128)}) fusion(s32[1,2]{1,0:T(1,128)} %param.7, s32[]{:T(128)S(6)} %select_n.30, s32[]{:T(128)S(6)} %select_n.27), kind=kLoop, calls=%fused_computation.53 | loop fusion | bytes 24 | tf_op jit(solution)/shard_map/jit(dynamic_index_in_dim)/dynamic_slice | solution.py:101
  4.9 1.5 %dynamic-slice_bitcast_fusion.1 = (bf16[1,64,6144]{2,1,0:T(8,128)(2,1)S(1)}, bf16[1,64,6144]{2,1,0:T(8,128)(2,1)S(1)}) fusion(bf16[1,2,64,6144]{3,2,1,0:T(8,128)(2,1)} %param.4, s32[]{:T(128)S(6)} %select_n.28, s32[]{:T(128)S(6)} %select_n.29), kind=kLoop, calls=%fused_computation.34 | loop fusion | bytes 3145736 | tf_op jit(solution)/shard_map/jit(dynamic_index_in_dim)/dynamic_slice | solution.py:107
  6.3 0.6 collective-permute-start
  7.6 0.0 copy-done
  7.6 0.2 reduce_window_sum.14
  8.4 0.1 pad_add_fusion
  8.5 0.0 copy-done.1
  8.5 0.2 select_reduce_fusion
  8.7 0.7 fusion.38
  9.4 0.6 compare_convert_fusion.1
  10.0 0.1 fusion.30
  10.1 0.1 multiply_reduce_fusion
  10.2 0.1 convert_reduce_fusion
  10.3 0.0 collective-permute-done
  10.3 0.2 reshape_reshape_broadcast_in_dim_reshape.6
  10.5 0.2 reshape_reshape_broadcast_in_dim_reshape.7
  10.7 0.2 pad_maximum_fusion.2
  10.9 0.9 copy.54
  11.8 4.7 %all-to-all-start = ((bf16[2,64,4,512]{3,1,0,2:T(8,128)(2,1)}), bf16[2,64,4,512]{3,1,0,2:T(8,128)(2,1)S(1)}, u32[]{:S(2)}, u32[]{:S(2)}) async-start(bf16[2,64,4,512]{3,1,0,2:T(8,128)(2,1)} %copy.54), calls=%async_computation | async-start | bytes 1048576 | tf_op jit(solution)/shard_map/all_to_all | solution.py:50
  16.5 0.1 pad_maximum_fusion
  16.6 1.1 %copy.88 = bf16[2,8,4,8,1024]{4,3,1,0,2:T(8,128)(2,1)} copy(bf16[2,8,4,8,1024]{4,3,2,1,0:T(8,128)(2,1)S(1)} %bitcast.113) | data formatting | bytes 2097152 | tf_op jit(solution)/shard_map/reshape | solution.py:39
  17.7 7.5 %all-to-all-done = bf16[2,64,4,512]{3,1,0,2:T(8,128)(2,1)S(1)} async-done(((bf16[2,64,4,512]{3,1,0,2:T(8,128)(2,1)}), bf16[2,64,4,512]{3,1,0,2:T(8,128)(2,1)S(1)}, u32[]{:S(2)}, u32[]{:S(2)}) %all-to-all-start) | async-done | bytes 524320 | tf_op jit(solution)/shard_map/all_to_all | solution.py:50
  25.2 3.5 %all-to-all-start.1 = ((bf16[2,64,4,1024]{3,1,0,2:T(8,128)(2,1)}), bf16[2,64,4,1024]{3,1,0,2:T(8,128)(2,1)S(1)}, u32[]{:S(2)}, u32[]{:S(2)}) async-start(bf16[2,64,4,1024]{3,1,0,2:T(8,128)(2,1)} %bitcast.111), calls=%async_computation.1 | async-start | bytes 2097152 | tf_op jit(solution)/shard_map/all_to_all | solution.py:49
  28.7 0.7 compare_convert_fusion
  29.4 0.1 fusion.29
  29.6 0.1 fusion.28
  29.8 0.1 copy.57
  29.9 0.1 copy.56
  30.0 0.1 copy.64
  30.1 0.1 copy.63
  30.2 12.0 %all-to-all-done.1 = bf16[2,64,4,1024]{3,1,0,2:T(8,128)(2,1)S(1)} async-done(((bf16[2,64,4,1024]{3,1,0,2:T(8,128)(2,1)}), bf16[2,64,4,1024]{3,1,0,2:T(8,128)(2,1)S(1)}, u32[]{:S(2)}, u32[]{:S(2)}) %all-to-all-start.1) | async-done | bytes 1048608 | tf_op jit(solution)/shard_map/all_to_all | solution.py:49
  42.1 0.1 fusion.35
  42.2 0.4 reshape_squeeze.20
  42.6 0.5 fusion.26
  43.1 0.9 fusion.40
  44.0 0.3 fusion.14
  44.3 0.3 copy.62
  44.6 0.4 convert_element_type.63
  45.0 0.4 reshape_squeeze.23
  45.4 0.5 fusion.24
  45.8 0.9 fusion.39
  46.7 0.3 fusion.15
  47.1 0.3 copy.68
  47.4 0.4 convert_element_type.67
  47.8 0.1 pad_maximum_fusion.1
  47.9 0.1 copy.69
  47.9 16.1 %all_to_all.51 = bf16[2,4,64,1024]{3,2,0,1:T(8,128)(2,1)S(1)} all-to-all(bf16[2,4,64,1024]{3,2,0,1:T(8,128)(2,1)S(1)} %copy.69), channel_id=1, replica_groups=mesh['section'=4,'dp'=2,'seq'=4] {'seq'}, dimensions={1} | all-to-all | bytes 2097152 | tf_op jit(solution)/shard_map/all_to_all | solution.py:114
  64.0 0.1 copy.82
  64.1 1.6 %collective-permute-start.1 = (bf16[2,1,64,4096]{3,2,0,1:T(8,128)(2,1)S(1)}, bf16[2,1,64,4096]{3,2,0,1:T(8,128)(2,1)S(1)}, u32[]{:S(2)}, u32[]{:S(2)}) collective-permute-start(bf16[2,1,64,4096]{3,2,0,1:T(8,128)(2,1)S(1)} %bitcast.116), channel_id=1, source_target_pairs={{0,8},{8,16},{16,24},{24,0},{1,9},{9,17},{17,25},{25,1},{2,10},{10... | collective-permute-start | bytes 3145736 | tf_op jit(solution)/shard_map/ppermute | solution.py:26
  65.7 22.9 %collective-permute-done.1 = bf16[2,1,64,4096]{3,2,0,1:T(8,128)(2,1)S(1)} collective-permute-done((bf16[2,1,64,4096]{3,2,0,1:T(8,128)(2,1)S(1)}, bf16[2,1,64,4096]{3,2,0,1:T(8,128)(2,1)S(1)}, u32[]{:S(2)}, u32[]{:S(2)}) %collective-permute-start.1) | collective-permute-done | bytes 1048608 | tf_op jit(solution)/shard_map/ppermute | solution.py:26
  88.7 1.0 %copy.90 = bf16[1,2,64,4096]{3,2,1,0:T(8,128)(2,1)} copy(bf16[1,2,64,4096]{3,2,1,0:T(8,128)(2,1)S(1)} %bitcast.117) | data formatting | bytes 2097152
  (4 shorter events, 0.1 us)
Async XLA Ops:
  0.0 7.6 %copy-start = (s32[1,4,8]{2,1,0:T(4,128)S(1)}, s32[1,4,8]{2,1,0:T(4,128)}, u32[]{:S(2)}) copy-start(s32[1,4,8]{2,1,0:T(4,128)} %param.6) | copy-start | bytes 388
  0.0 8.5 %copy-start.1 = (s32[1,4]{1,0:T(1,128)S(1)}, s32[1,4]{1,0:T(1,128)}, u32[]{:S(2)}) copy-start(s32[1,4]{1,0:T(1,128)} %param.5) | copy-start | bytes 52
  6.3 3.9 %collective-permute-start = (bf16[1,64,6144]{2,1,0:T(8,128)(2,1)S(1)}, bf16[1,64,6144]{2,1,0:T(8,128)(2,1)S(1)}, u32[]{:S(2)}, u32[]{:S(2)}) collective-permute-start(bf16[1,64,6144]{2,1,0:T(8,128)(2,1)S(1)} %get-tuple-element.8), channel_id=1, source_target_pairs={{0,4},{4,0},{1,5},{5,1},{2,6},{6,2},{3,7},{7,3},{8,12},{12,8},{9,1... | collective-permute-start | bytes 2359304 | tf_op jit(solution)/shard_map/ppermute | solution.py:20
  11.8 13.4 %all-to-all-start = ((bf16[2,64,4,512]{3,1,0,2:T(8,128)(2,1)}), bf16[2,64,4,512]{3,1,0,2:T(8,128)(2,1)S(1)}, u32[]{:S(2)}, u32[]{:S(2)}) async-start(bf16[2,64,4,512]{3,1,0,2:T(8,128)(2,1)} %copy.54), calls=%async_computation | async-start | bytes 1048576 | tf_op jit(solution)/shard_map/all_to_all | solution.py:50
  25.2 16.9 %all-to-all-start.1 = ((bf16[2,64,4,1024]{3,1,0,2:T(8,128)(2,1)}), bf16[2,64,4,1024]{3,1,0,2:T(8,128)(2,1)S(1)}, u32[]{:S(2)}, u32[]{:S(2)}) async-start(bf16[2,64,4,1024]{3,1,0,2:T(8,128)(2,1)} %bitcast.111), calls=%async_computation.1 | async-start | bytes 2097152 | tf_op jit(solution)/shard_map/all_to_all | solution.py:49
  64.1 24.6 %collective-permute-start.1 = (bf16[2,1,64,4096]{3,2,0,1:T(8,128)(2,1)S(1)}, bf16[2,1,64,4096]{3,2,0,1:T(8,128)(2,1)S(1)}, u32[]{:S(2)}, u32[]{:S(2)}) collective-permute-start(bf16[2,1,64,4096]{3,2,0,1:T(8,128)(2,1)S(1)} %bitcast.116), channel_id=1, source_target_pairs={{0,8},{8,16},{16,24},{24,0},{1,9},{9,17},{17,25},{25,1},{2,10},{10... | collective-permute-start | bytes 3145736 | tf_op jit(solution)/shard_map/ppermute | solution.py:26
where the time goes:
time: 90 us; the launch traced here: 89.6 us
  waiting for transfers between devices  42.4 us (47%)
  blocking collectives  16.1 us (18%)
  starting transfers between devices  10.4 us (12%)
  local copies, waits for them, and re-layouts  9.62 us (11%)
  between operations  5.03 us (6%)
  other arithmetic  4.47 us (5%)
  matrix products  1.61 us (2%)
    ppermute x1, waiting for transfers between devices, passed_along(): return lax.ppermute(value, axis, pairs)  22.9 us
    all_to_all x1, blocking collectives, shards(): lax.all_to_all(grouped, 'seq', split_axis=1, concat_axis=3, tiled=True)  16.1 us
    all_to_all x1, waiting for transfers between devices, attend(): lax.all_to_all(query_send, 'seq', split_axis=2, concat_axis=1, tiled=True)  12 us
    all_to_all x1, waiting for transfers between devices, attend(): lax.all_to_all(jnp.concatenate([key_send, value_send], axis=3), 'seq', sp...  7.52 us
    all_to_all x1, starting transfers between devices, attend(): lax.all_to_all(jnp.concatenate([key_send, value_send], axis=3), 'seq', sp...  4.71 us
    all_to_all x1, starting transfers between devices, attend(): lax.all_to_all(query_send, 'seq', split_axis=2, concat_axis=1, tiled=True)  3.52 us
  transfers between devices with their start and end apart: 4, of which 3 were waited for; matrix products, arithmetic and copies ran while one was open for 5% of the time, Pallas kernels for 0%

commit v1 on v0

--- a/solution.py
+++ b/solution.py
@@ -47,12 +47,20 @@
     )
     query_heads, kv_heads = (
         lax.all_to_all(query_send, "seq", split_axis=2, concat_axis=1, tiled=True),
-        lax.all_to_all(
-            jnp.concatenate([key_send, value_send], axis=3),
-            "seq",
-            split_axis=2,
-            concat_axis=1,
-            tiled=True,
+        jnp.concatenate(
+            lax.all_to_all(
+                jnp.stack(
+                    jnp.split(
+                        jnp.concatenate([key_send, value_send], axis=3),
+                        lax.axis_size("seq"),
+                        axis=2,
+                    )
+                ),
+                "seq",
+                0,
+                0,
+            ),
+            axis=1,
         ),
     )
     key_block = kv_heads[:, :, 0, : kv_dev * HD]

time: 90 us -> 90.9 us (1.010)
  no operation moved by 1% of the time
where the time goes in v1:
time: 90.9 us; the launch traced here: 90.5 us
  waiting for transfers between devices  42.4 us (47%)
  blocking collectives  16.1 us (18%)
  starting transfers between devices  10.4 us (11%)
  local copies, waits for them, and re-layouts  9.82 us (11%)
  other arithmetic  5.1 us (6%)
  between operations  5.06 us (6%)
  matrix products  1.61 us (2%)
    ppermute x1, waiting for transfers between devices, passed_along(): return lax.ppermute(value, axis, pairs)  22.9 us
    all_to_all x1, blocking collectives, shards(): lax.all_to_all(grouped, 'seq', split_axis=1, concat_axis=3, tiled=True)  16.1 us
    all_to_all x1, waiting for transfers between devices, attend(): lax.all_to_all(query_send, 'seq', split_axis=2, concat_axis=1, tiled=True)  12 us
    all_to_all x1, waiting for transfers between devices, attend(): lax.all_to_all(jnp.stack(jnp.split(jnp.concatenate([key_send, value_send]...  7.52 us
    all_to_all x1, starting transfers between devices, attend(): lax.all_to_all(jnp.stack(jnp.split(jnp.concatenate([key_send, value_send]...  4.71 us
    all_to_all x1, starting transfers between devices, attend(): lax.all_to_all(query_send, 'seq', split_axis=2, concat_axis=1, tiled=True)  3.52 us
  transfers between devices with their start and end apart: 4, of which 3 were waited for; matrix products, arithmetic and copies ran while one was open for 5% of the time, Pallas kernels for 0%

profile of v1, /device:TPU:0, one launch (start us, length us, event | category | flops | bytes accessed | tf_op | source)
XLA Modules:
  0.0 90.5 jit_solution(7274897276272407798)
XLA Ops:
  0.0 0.0 copy-start
  0.0 0.0 copy-start.1
  0.0 1.4 %constant_dynamic-slice_fusion = (s32[1,1]{1,0:T(1,128)}, s32[1,1]{1,0:T(1,128)}) fusion(s32[1,2]{1,0:T(1,128)} %param.7, s32[]{:T(128)S(6)} %select_n.30, s32[]{:T(128)S(6)} %select_n.27), kind=kLoop, calls=%fused_computation.59 | loop fusion | bytes 24 | tf_op jit(solution)/shard_map/jit(dynamic_index_in_dim)/dynamic_slice | solution.py:109
  4.9 1.5 %dynamic-slice_bitcast_fusion.1 = (bf16[1,64,6144]{2,1,0:T(8,128)(2,1)S(1)}, bf16[1,64,6144]{2,1,0:T(8,128)(2,1)S(1)}) fusion(bf16[1,2,64,6144]{3,2,1,0:T(8,128)(2,1)} %param.4, s32[]{:T(128)S(6)} %select_n.28, s32[]{:T(128)S(6)} %select_n.29), kind=kLoop, calls=%fused_computation.34 | loop fusion | bytes 3145736 | tf_op jit(solution)/shard_map/jit(dynamic_index_in_dim)/dynamic_slice | solution.py:115
  6.3 0.6 collective-permute-start
  7.6 0.0 copy-done
  7.6 0.2 reduce_window_sum.14
  8.4 0.1 pad_add_fusion
  8.5 0.0 copy-done.1
  8.5 0.2 select_reduce_fusion
  8.7 0.7 fusion.39
  9.4 0.6 compare_convert_fusion.1
  10.0 0.1 fusion.30
  10.1 0.1 multiply_reduce_fusion
  10.2 0.1 convert_reduce_fusion
  10.3 0.0 collective-permute-done
  10.3 0.2 reshape_reshape_broadcast_in_dim_reshape.6
  10.5 0.1 constant_dynamic-update-slice_fusion.1
  10.6 0.2 reshape_reshape_broadcast_in_dim_reshape.7
  10.8 0.1 constant_dynamic-update-slice_fusion
  10.9 0.8 fusion.37
  11.8 0.9 pad_maximum_fusion.2
  12.7 4.7 %all-to-all-start = ((bf16[4,2,64,1,512]{4,2,1,3,0:T(8,128)(2,1)}), bf16[4,2,64,1,512]{4,2,1,3,0:T(8,128)(2,1)S(1)}, u32[]{:S(2)}, u32[]{:S(2)}) async-start(bf16[4,2,64,1,512]{4,2,1,3,0:T(8,128)(2,1)} %pad_maximum_fusion.2), calls=%async_computation | async-start | bytes 1048576 | tf_op jit(solution)/shard_map/all_to_all | solution.py:51
  17.4 0.1 pad_maximum_fusion
  17.5 1.1 %copy.132 = bf16[2,8,4,8,1024]{4,3,1,0,2:T(8,128)(2,1)} copy(bf16[2,8,4,8,1024]{4,3,2,1,0:T(8,128)(2,1)S(1)} %bitcast.118) | data formatting | bytes 2097152 | tf_op jit(solution)/shard_map/reshape | solution.py:39
  18.6 7.5 %all-to-all-done = bf16[4,2,64,1,512]{4,2,1,3,0:T(8,128)(2,1)S(1)} async-done(((bf16[4,2,64,1,512]{4,2,1,3,0:T(8,128)(2,1)}), bf16[4,2,64,1,512]{4,2,1,3,0:T(8,128)(2,1)S(1)}, u32[]{:S(2)}, u32[]{:S(2)}) %all-to-all-start) | async-done | bytes 524320 | tf_op jit(solution)/shard_map/all_to_all | solution.py:51
  26.1 3.5 %all-to-all-start.1 = ((bf16[2,64,4,1024]{3,1,0,2:T(8,128)(2,1)}), bf16[2,64,4,1024]{3,1,0,2:T(8,128)(2,1)S(1)}, u32[]{:S(2)}, u32[]{:S(2)}) async-start(bf16[2,64,4,1024]{3,1,0,2:T(8,128)(2,1)} %bitcast.116), calls=%async_computation.1 | async-start | bytes 2097152 | tf_op jit(solution)/shard_map/all_to_all | solution.py:49
  29.6 0.7 compare_convert_fusion
  30.3 0.1 fusion.29
  30.4 0.1 fusion.28
  30.6 0.1 copy.93
  30.7 0.1 copy.92
  30.8 0.1 copy.100
  30.9 0.1 copy.99
  31.0 12.0 %all-to-all-done.1 = bf16[2,64,4,1024]{3,1,0,2:T(8,128)(2,1)S(1)} async-done(((bf16[2,64,4,1024]{3,1,0,2:T(8,128)(2,1)}), bf16[2,64,4,1024]{3,1,0,2:T(8,128)(2,1)S(1)}, u32[]{:S(2)}, u32[]{:S(2)}) %all-to-all-start.1) | async-done | bytes 1048608 | tf_op jit(solution)/shard_map/all_to_all | solution.py:49
  43.0 0.1 fusion.35
  43.1 0.4 reshape_squeeze.20
  43.5 0.5 fusion.26
  43.9 0.9 fusion.41
  44.8 0.3 fusion.14
  45.2 0.3 copy.98
  45.5 0.4 convert_element_type.63
  45.9 0.4 reshape_squeeze.23
  46.2 0.5 fusion.24
  46.7 0.9 fusion.40
  47.6 0.3 fusion.15
  47.9 0.3 copy.104
  48.3 0.4 convert_element_type.67
  48.6 0.1 pad_maximum_fusion.1
  48.7 0.1 copy.105
  48.8 16.1 %all_to_all.38 = bf16[2,4,64,1024]{3,2,0,1:T(8,128)(2,1)S(1)} all-to-all(bf16[2,4,64,1024]{3,2,0,1:T(8,128)(2,1)S(1)} %copy.105), channel_id=1, replica_groups=mesh['section'=4,'dp'=2,'seq'=4] {'seq'}, dimensions={1} | all-to-all | bytes 2097152 | tf_op jit(solution)/shard_map/all_to_all | solution.py:122
  64.9 0.1 copy.122
  65.0 1.6 %collective-permute-start.1 = (bf16[2,1,64,4096]{3,2,0,1:T(8,128)(2,1)S(1)}, bf16[2,1,64,4096]{3,2,0,1:T(8,128)(2,1)S(1)}, u32[]{:S(2)}, u32[]{:S(2)}) collective-permute-start(bf16[2,1,64,4096]{3,2,0,1:T(8,128)(2,1)S(1)} %bitcast.122), channel_id=1, source_target_pairs={{0,8},{8,16},{16,24},{24,0},{1,9},{9,17},{17,25},{25,1},{2,10},{10... | collective-permute-start | bytes 3145736 | tf_op jit(solution)/shard_map/ppermute | solution.py:26
  66.6 22.9 %collective-permute-done.1 = bf16[2,1,64,4096]{3,2,0,1:T(8,128)(2,1)S(1)} collective-permute-done((bf16[2,1,64,4096]{3,2,0,1:T(8,128)(2,1)S(1)}, bf16[2,1,64,4096]{3,2,0,1:T(8,128)(2,1)S(1)}, u32[]{:S(2)}, u32[]{:S(2)}) %collective-permute-start.1) | collective-permute-done | bytes 1048608 | tf_op jit(solution)/shard_map/ppermute | solution.py:26
  89.5 1.0 %copy.135 = bf16[1,2,64,4096]{3,2,1,0:T(8,128)(2,1)} copy(bf16[1,2,64,4096]{3,2,1,0:T(8,128)(2,1)S(1)} %bitcast.123) | data formatting | bytes 2097152
  (6 shorter events, 0.2 us)
Async XLA Ops:
  0.0 7.6 %copy-start = (s32[1,4,8]{2,1,0:T(4,128)S(1)}, s32[1,4,8]{2,1,0:T(4,128)}, u32[]{:S(2)}) copy-start(s32[1,4,8]{2,1,0:T(4,128)} %param.6) | copy-start | bytes 388
  0.0 8.5 %copy-start.1 = (s32[1,4]{1,0:T(1,128)S(1)}, s32[1,4]{1,0:T(1,128)}, u32[]{:S(2)}) copy-start(s32[1,4]{1,0:T(1,128)} %param.5) | copy-start | bytes 52
  6.3 3.9 %collective-permute-start = (bf16[1,64,6144]{2,1,0:T(8,128)(2,1)S(1)}, bf16[1,64,6144]{2,1,0:T(8,128)(2,1)S(1)}, u32[]{:S(2)}, u32[]{:S(2)}) collective-permute-start(bf16[1,64,6144]{2,1,0:T(8,128)(2,1)S(1)} %get-tuple-element.8), channel_id=1, source_target_pairs={{0,4},{4,0},{1,5},{5,1},{2,6},{6,2},{3,7},{7,3},{8,12},{12,8},{9,1... | collective-permute-start | bytes 2359304 | tf_op jit(solution)/shard_map/ppermute | solution.py:20
  12.7 13.4 %all-to-all-start = ((bf16[4,2,64,1,512]{4,2,1,3,0:T(8,128)(2,1)}), bf16[4,2,64,1,512]{4,2,1,3,0:T(8,128)(2,1)S(1)}, u32[]{:S(2)}, u32[]{:S(2)}) async-start(bf16[4,2,64,1,512]{4,2,1,3,0:T(8,128)(2,1)} %pad_maximum_fusion.2), calls=%async_computation | async-start | bytes 1048576 | tf_op jit(solution)/shard_map/all_to_all | solution.py:51
  26.1 16.9 %all-to-all-start.1 = ((bf16[2,64,4,1024]{3,1,0,2:T(8,128)(2,1)}), bf16[2,64,4,1024]{3,1,0,2:T(8,128)(2,1)S(1)}, u32[]{:S(2)}, u32[]{:S(2)}) async-start(bf16[2,64,4,1024]{3,1,0,2:T(8,128)(2,1)} %bitcast.116), calls=%async_computation.1 | async-start | bytes 2097152 | tf_op jit(solution)/shard_map/all_to_all | solution.py:49
  65.0 24.5 %collective-permute-start.1 = (bf16[2,1,64,4096]{3,2,0,1:T(8,128)(2,1)S(1)}, bf16[2,1,64,4096]{3,2,0,1:T(8,128)(2,1)S(1)}, u32[]{:S(2)}, u32[]{:S(2)}) collective-permute-start(bf16[2,1,64,4096]{3,2,0,1:T(8,128)(2,1)S(1)} %bitcast.122), channel_id=1, source_target_pairs={{0,8},{8,16},{16,24},{24,0},{1,9},{9,17},{17,25},{25,1},{2,10},{10... | collective-permute-start | bytes 3145736 | tf_op jit(solution)/shard_map/ppermute | solution.py:26
